TPU v7x, 256 devices: a whole 4x4x8 slice. The times are simulated.
256 devices in a mesh: bank: 64 (over x, z, core), dp: 4 (over y).
Axes of the slice: x: 4, y: 4, z: 8, core: 2. Of those that a mesh axis runs over, the one named last changes fastest.
Arguments:
- event_features: bfloat16 [4096, 16, 128], P(('bank', 'dp')), may hold values from -6 to 6
- event_bins: int32 [4096, 16], P(('bank', 'dp')), may hold values from 0 to 7
- positive: int32 [4096], P(('bank', 'dp')), may hold values from 0 to 131071
- teacher_bank: bfloat16 [131072, 1024], P('bank'), may hold values from -16 to 16
- in_weight: bfloat16 [128, 512], replicated, may hold values from -0.5 to 0.5
- embedding_head_weight: bfloat16 [512, 1024], replicated, may hold values from -1 to 1
- membrane_decay_rate: float32 [512], replicated, may hold values from 0.3 to 0.95
Outputs:
- sample_loss: float32 [4096], P(('bank', 'dp'))
- in_grad: float32 [128, 512], P('bank')
- head_weight_gradient: float32 [512, 1024], P('bank')
All inputs are finite; a program needn't handle non-finite values.
Results may differ from a plain program's by a relative error of at most 0.0042.
Values may be sent and summed in bfloat16 or wider, within the bound.
No kernel may reach another device: no remote copies, remote signals or barrier semaphores. Data moves between devices by JAX's collectives and lax.ppermute only.
A program may use at most 64 MiB of HBM per device.

v0:
```python
from functools import partial

import jax
import jax.numpy as jnp
from jax import lax
from jax.sharding import PartitionSpec as P

D = 1024
H = 512
C_IN = 128
TIME = 8


sharpening_divisor = 0.07
objective_divisor = 64.0
threshold = 1.0
sharpness = 4.0
epsilon = 1e-06


def membrane_potential(input_current, membrane_decay_rate):
    potential = jnp.zeros((input_current.shape[0], input_current.shape[2]), jnp.float32)
    spikes = jnp.zeros_like(potential)
    totals = jnp.zeros_like(potential)
    for moment in range(input_current.shape[1]):
        potential = membrane_decay_rate * potential + input_current[:, moment, :] - spikes
        spikes = jax.nn.sigmoid(sharpness * (potential - threshold))
        totals = totals + spikes
    return totals / input_current.shape[1]


def body(
    event_features,
    event_bins,
    positive,
    teacher_bank,
    in_weight,
    embedding_head_weight,
    membrane_decay_rate,
):
    per_device = positive.shape[0]
    bank_rows = teacher_bank.shape[0]
    onehot = (event_bins[:, None, :] == jnp.arange(TIME, dtype=jnp.int32)[None, :, None]).astype(
        jnp.bfloat16
    )
    binned = jnp.einsum(
        "ste,sec->stc", onehot, event_features, preferred_element_type=jnp.float32
    ).astype(jnp.bfloat16)
    flat_in = binned.reshape(per_device * TIME, C_IN)
    input_current = jnp.dot(flat_in, in_weight, preferred_element_type=jnp.float32).reshape(
        per_device, TIME, H
    )
    spike_train, leaky_neuron_backward = jax.vjp(
        partial(membrane_potential, membrane_decay_rate=membrane_decay_rate), input_current
    )
    spike_train_reduced = spike_train.astype(jnp.bfloat16)
    projected_embedding = jnp.dot(
        spike_train_reduced, embedding_head_weight, preferred_element_type=jnp.float32
    )
    length = jnp.sqrt(
        jnp.sum(projected_embedding * projected_embedding, axis=1, keepdims=True) + epsilon
    )
    query = projected_embedding / length
    query_low = query.astype(jnp.bfloat16)
    gathered, gathered_pos = (
        lax.all_gather(query_low, "bank", axis=0, tiled=True),
        lax.all_gather(positive, "bank", axis=0, tiled=True),
    )
    position = lax.axis_index("bank")
    start_row = position * bank_rows
    inverse = 1.0 / jnp.sqrt(
        jnp.sum(jnp.square(teacher_bank.astype(jnp.float32)), axis=1) + epsilon
    )
    local_index = gathered_pos - start_row
    is_owner = (local_index >= 0) & (local_index < bank_rows)
    local_index = jnp.clip(local_index, 0, bank_rows - 1)
    total_rows = gathered.shape[0]
    block = min(512, total_rows)
    block_count = total_rows // block

    def score_block(block_item):
        block_query, block_local, block_owner = block_item
        cosine_affinity_matrix = (
            jnp.dot(block_query, teacher_bank.T, preferred_element_type=jnp.float32)
            * inverse[None, :]
            / sharpening_divisor
        )
        exponent = jnp.exp(cosine_affinity_matrix)
        weights = (exponent * inverse[None, :]).astype(jnp.bfloat16)
        picked = jnp.take_along_axis(cosine_affinity_matrix, block_local[:, None], axis=1)[:, 0]
        return (jnp.sum(exponent, axis=1), jnp.where(block_owner, picked, 0.0), weights)

    partition_part, pos_part, weights = lax.map(
        score_block,
        (
            gathered.reshape(block_count, block, D),
            local_index.reshape(block_count, block),
            is_owner.reshape(block_count, block),
        ),
    )
    partition_part = partition_part.reshape(total_rows)
    pos_part = pos_part.reshape(total_rows)
    weights = weights.reshape(total_rows, bank_rows)
    exponent_total, matched_dot_value = lax.psum((partition_part, pos_part), "bank")
    own_partition = lax.dynamic_slice_in_dim(exponent_total, position * per_device, per_device, 0)
    own_pos = lax.dynamic_slice_in_dim(matched_dot_value, position * per_device, per_device, 0)
    sample_loss = jnp.log(own_partition) - own_pos
    partial_sums = jnp.dot(weights, teacher_bank, preferred_element_type=jnp.float32)
    matched_entries = (
        jnp.take(teacher_bank, local_index, axis=0).astype(jnp.float32)
        * jnp.take(inverse, local_index)[:, None]
    )
    local_owned_rows = jnp.where(is_owner[:, None], matched_entries, 0.0)
    query_grad = lax.psum_scatter(
        (partial_sums / exponent_total[:, None] - local_owned_rows)
        / (sharpening_divisor * objective_divisor),
        "bank",
        scatter_dimension=0,
        tiled=True,
    )
    projection_gradient = (
        (query_grad - query * jnp.sum(query * query_grad, axis=1, keepdims=True)) / length
    ).astype(jnp.bfloat16)
    head_weight_piece = jnp.dot(
        spike_train_reduced.T, projection_gradient, preferred_element_type=jnp.float32
    )
    spike_train_gradient = jnp.dot(
        projection_gradient, embedding_head_weight.T, preferred_element_type=jnp.float32
    )
    (input_current_gradient,) = leaky_neuron_backward(spike_train_gradient)
    current_low = input_current_gradient.astype(jnp.bfloat16).reshape(per_device * TIME, H)
    in_part = jnp.dot(flat_in.T, current_low, preferred_element_type=jnp.float32)
    bank_size = lax.axis_size("bank")
    in_share_rows = C_IN // bank_size
    head_share_rows = H // bank_size
    in_full, head_full = lax.psum((in_part, head_weight_piece), ("bank", "dp"))
    in_grad = lax.dynamic_slice_in_dim(in_full, position * in_share_rows, in_share_rows, 0)
    head_weight_gradient = lax.dynamic_slice_in_dim(
        head_full, position * head_share_rows, head_share_rows, 0
    )
    return (sample_loss, in_grad, head_weight_gradient)


def solution(mesh):
    in_specs = (
        P(("bank", "dp"), None, None),
        P(("bank", "dp"), None),
        P(("bank", "dp")),
        P("bank", None),
        P(),
        P(),
        P(),
    )
    out_specs = (P(("bank", "dp")), P("bank", None), P("bank", None))
    return jax.shard_map(body, mesh=mesh, in_specs=in_specs, out_specs=out_specs, check_vma=False)
```

profile of v0, /device:TPU:2, one launch (start us, length us, event | category | flops | bytes accessed | tf_op | source)
XLA Modules:
  0.0 687.4 jit_solution(5577783720457699352)
XLA Ops:
  7.2 0.0 copy-start
  7.2 0.0 all-gather.2.cloned.1.call-start
  7.2 1.1 convolution_convert_fusion
  8.3 1.1 fusion.8
  9.4 0.2 fusion.67
  9.6 0.7 broadcast_multiply_fusion
  10.3 0.8 fusion.35
  11.1 0.0 copy-done
  11.1 1.1 multiply_reduce_fusion.2
  12.2 0.7 fusion.59
  12.9 0.0 all-gather.2.cloned.1.call-update
  12.9 0.0 reduce-scatter.2.cloned.1.call-start
  13.0 1.3 dynamic-slice
  14.9 0.9 dynamic-update-slice
  15.8 22.5 %all-reduce.8 = s32[1024]{0:T(1024)S(1)} all-reduce(s32[1024]{0:T(1024)S(1)} %dynamic-update-slice), channel_id=1, replica_groups=mesh['bank'=64,'dp'=4] {'bank'}, use_global_device_ids=true, to_apply=%add.8 | all-reduce | flops 1024 | bytes 8192
  38.3 0.0 copy-start.2
  38.3 0.5 copy-done.2
  38.8 7.7 %gather_fusion.1 = bf16[1024,1024]{1,0:T(8,128)(2,1)S(1)} fusion(bf16[2048,1024]{1,0:T(8,128)(2,1)} %param.12, s32[1024]{0:T(1024)S(1)} %get-tuple-element.85), kind=kCustom, calls=%fused_computation.1 | custom fusion | bytes 4198400 | tf_op jit(solution)/shard_map/jit(_take)/gather | solution.py:110
  46.6 3.1 multiply_reduce_fusion
  49.7 6.2 gather_fusion.2
  55.8 0.6 broadcast_select_fusion
  56.4 36.1 %all-gather.2.cloned.1.call-done = bf16[1024,1024]{1,0:T(8,128)(2,1)} async-done(((bf16[16,1024]{1,0:T(8,128)(2,1)}), bf16[1024,1024]{1,0:T(8,128)(2,1)}) %all-gather.2.cloned.1.call-update) | async-done | bytes 2097168 | tf_op jit(solution)/shard_map/all_gather | solution.py:66
  92.4 39.1 %while.14 = (s32[]{:T(128)}, f32[2,512]{1,0:T(2,128)S(1)}, f32[2,512]{1,0:T(2,128)S(1)}, bf16[2,512,2048]{2,1,0:T(8,128)(2,1)}, bf16[2,512,1024]{2,1,0:T(8,128)(...) while((s32[]{:T(128)}, f32[2,512]{1,0:T(2,128)S(1)}, ...), condition=%wide.region_4.5_spmd, body=%wide.region_2.4_spmd.sunk | while | flops 2152735232 | bytes 15790733 | solution.py:93
  92.4 7.1 %exponential_reduce_fusion.2 = (f32[512]{0:T(512)S(1)}, f32[512,2048]{1,0:T(8,128)}) fusion(f32[2048]{0:T(1024)S(1)} %get-tuple-element.192, bf16[2048,1024]{1,0:T(8,128)(2,1)} %get-tuple-element.191, bf16[2,512,1024]{2,1,0:T(8,128)(2,1)} %get-tuple-element.190, s32[]{:T(128)S(6)} %copy.174), kind=kOutput, calls=%fused_computation.5.clone.1 | convolution fusion | flops 2150628864 | bytes 9447428 | tf_op jit(solution)/shard_map/while/body/eval_jaxpr/dot_general | solution.py:84
  99.6 8.1 %gather_fusion = f32[512]{0:T(512)S(1)} fusion(f32[512,2048]{1,0:T(8,128)} %get-tuple-element.163, s32[512]{0:T(512)S(1)} %bitcast.213), kind=kCustom, calls=%fused_computation.clone.1 | custom fusion | bytes 8192 | tf_op jit(solution)/shard_map/while/body/eval_jaxpr/jit(take_along_axis)/gather | solution.py:90
  107.7 4.2 fusion.81
  111.9 7.1 %exponential_reduce_fusion.2 = (f32[512]{0:T(512)S(1)}, f32[512,2048]{1,0:T(8,128)}) fusion(f32[2048]{0:T(1024)S(1)} %get-tuple-element.192, bf16[2048,1024]{1,0:T(8,128)(2,1)} %get-tuple-element.191, bf16[2,512,1024]{2,1,0:T(8,128)(2,1)} %get-tuple-element.190, s32[]{:T(128)S(6)} %copy.174), kind=kOutput, calls=%fused_computation.5.clone.1 | convolution fusion | flops 2150628864 | bytes 9447428 | tf_op jit(solution)/shard_map/while/body/eval_jaxpr/dot_general | solution.py:84
  119.1 8.1 %gather_fusion = f32[512]{0:T(512)S(1)} fusion(f32[512,2048]{1,0:T(8,128)} %get-tuple-element.163, s32[512]{0:T(512)S(1)} %bitcast.213), kind=kCustom, calls=%fused_computation.clone.1 | custom fusion | bytes 8192 | tf_op jit(solution)/shard_map/while/body/eval_jaxpr/jit(take_along_axis)/gather | solution.py:90
  127.3 4.2 fusion.81
  131.5 109.4 %all-reduce.10 = (f32[1024]{0:T(1024)S(1)}, f32[1024]{0:T(1024)S(1)}) all-reduce(f32[1024]{0:T(1024)S(1)} %bitcast.219, f32[1024]{0:T(1024)S(1)} %bitcast.220), channel_id=1, replica_groups=mesh['bank'=64,'dp'=4] {'bank'}, use_global_device_ids=true, to_apply=%region_6.7 | all-reduce | flops 2048 | bytes 16384 | tf_op jit(solution)/shard_map/psum | solution.py:104
  240.9 9.6 %subtract_multiply_fusion = f32[1024,1024]{1,0:T(8,128)} fusion(bf16[1024,2048]{1,0:T(8,128)(2,1)} %bitcast.223, bf16[2048,1024]{1,0:T(8,128)(2,1)} %get-tuple-element.203, f32[1024]{0:T(1024)S(1)} %get-tuple-element.83, bf16[1024,1024]{1,0:T(8,128)(2,1)S(1)} %gather_fusion.1, f32[1024]{0:T(1024)S(1)} %get-tuple-element.76, ...), kind=kOutput, calls=%fused_computation.23 | convolution fusion | flops 4302307328 | bytes 14690304 | tf_op jit(solution)/shard_map/dot_general | solution.py:108
  250.5 0.0 reduce-scatter.2.cloned.1.call-update
  250.5 0.0 all-reduce.13.cloned.1.call-start
  250.6 158.8 %reduce-scatter.2.cloned.1.call-done = f32[16,1024]{1,0:T(8,128)} async-done(((f32[1024,1024]{1,0:T(8,128)}), f32[16,1024]{1,0:T(8,128)}) %reduce-scatter.2.cloned.1.call-update) | async-done | bytes 65552 | tf_op jit(solution)/shard_map/reduce_scatter | solution.py:114
  409.3 1.0 multiply_reduce_fusion.1
  410.4 1.2 convolution_multiply_fusion
  411.6 0.0 copy-done.1
  411.6 0.1 fusion.58
  411.7 0.1 fusion.57
  411.8 0.1 fusion.56
  411.9 0.1 fusion.33
  412.0 0.9 convolution_bitcast_fusion
  412.9 2.7 fusion.60
  415.6 0.0 all-reduce.13.cloned.1.call-update
  415.6 0.6 dynamic-slice_subtract_fusion
  416.2 261.9 %all-reduce.13.cloned.1.call-done = (f32[128,512]{1,0:T(8,128)}, f32[512,1024]{1,0:T(8,128)}) async-done(((f32[128,512]{1,0:T(8,128)}, f32[512,1024]{1,0:T(8,128)}), (f32[128,512]{1,0:T(8,128)}, f32[512,1024]{1,0:T(8,128)})) %all-reduce.13.cloned.1.call-update) | async-done | bytes 2359312 | tf_op jit(solution)/shard_map/psum | solution.py:136
  678.2 1.3 constant_dynamic-slice_fusion.2
  679.5 1.4 constant_dynamic-slice_fusion.1
  (28 shorter events, 0.3 us)
Async XLA Ops:
  7.2 3.9 copy-start
  7.2 85.3 %all-gather.2.cloned.1.call-start = ((), (), s32[]{:S(2)}) async-start(), calls=%async_computation.1 | async-start | bytes 2129920 | tf_op jit(solution)/shard_map/all_gather | solution.py:66
  12.9 396.4 %reduce-scatter.2.cloned.1.call-start = ((), (), s32[]{:S(2)}) async-start(), calls=%async_computation.2 | async-start | bytes 4259840 | tf_op jit(solution)/shard_map/reduce_scatter | solution.py:114
  38.3 0.6 copy-start.2
  250.5 161.1 %copy-start.1 = (f32[512]{0:T(512)S(1)}, f32[512]{0:T(512)}, u32[]{:S(2)}) copy-start(f32[512]{0:T(512)} %param.15) | copy-start | bytes 6148
  250.5 427.6 %all-reduce.13.cloned.1.call-start = ((), (), s32[]{:S(2)}) async-start(), calls=%async_computation.3 | async-start | bytes 4718592 | tf_op jit(solution)/shard_map/psum | solution.py:136
Sparse Core Ops, SparseCore 0:
  13.0 79.3 all-gather.1
  250.7 158.6 reduce-scatter.1
  415.7 262.3 all-reduce.12
where the time goes:
time: 689 us; the launch traced here: 687 us
  waiting for transfers between devices  457 us (66%)
  blocking collectives  132 us (19%)
  local copies, waits for them, and re-layouts  35.8 us (5%)
  matrix products  31.8 us (5%)
  other arithmetic  16.4 us (2%)
  between operations  14.6 us (2%)
    psum x1, waiting for transfers between devices, body(): in_full, head_full = lax.psum((in_part, head_weight_piece), ('bank', 'dp'))  262 us
    reduce_scatter x1, waiting for transfers between devices, body(): lax.psum_scatter((partial_sums / exponent_total[:, None] - local_owned_ro...  159 us
    psum x1, blocking collectives, body(): lax.psum((partition_part, pos_part), 'bank')  109 us
    all_gather x1, waiting for transfers between devices, body(): lax.all_gather(query_low, 'bank', axis=0, tiled=True)  36.1 us
    unnamed x1, blocking collectives  22.5 us
    gather x2, local copies, waits for them, and re-layouts, score_block(): jnp.take_along_axis(cosine_affinity_matrix, block_local[:, None], axis=1)  16.2 us
    dot_general x2, matrix products, score_block(): jnp.dot(block_query, teacher_bank.T, preferred_element_type=jnp.float32)  14.1 us
  transfers between devices with their start and end apart: 3, of which 3 were waited for; matrix products, arithmetic and copies ran while one was open for 3% of the time, Pallas kernels for 0%

commit v1 on v0

v1 whole, which is shorter than its diff:
```python
from functools import partial

import jax
import jax.numpy as jnp
from jax import lax
from jax.sharding import Mesh
from jax.sharding import PartitionSpec as P

D = 1024
H = 512
C_IN = 128
TIME = 8


sharpening_divisor = 0.07
objective_divisor = 64.0
threshold = 1.0
sharpness = 4.0
epsilon = 1e-06

BANK_AXES = ("bx", "bz", "bc")
SAMPLE_AXES = ("bx", "bz", "bc", "dp")
GATHER_ORDER = ("bx", "bz", "bc")
CODE_COLS = 128


def membrane_potential(input_current, membrane_decay_rate):
    potential = jnp.zeros((input_current.shape[0], input_current.shape[2]), jnp.float32)
    spikes = jnp.zeros_like(potential)
    totals = jnp.zeros_like(potential)
    for moment in range(input_current.shape[1]):
        potential = membrane_decay_rate * potential + input_current[:, moment, :] - spikes
        spikes = jax.nn.sigmoid(sharpness * (potential - threshold))
        totals = totals + spikes
    return totals / input_current.shape[1]


def gathered_block_index():
    index = 0
    for name in reversed(GATHER_ORDER):
        index = index * lax.axis_size(name) + lax.axis_index(name)
    return index


def bank_index():
    index = 0
    for name in BANK_AXES:
        index = index * lax.axis_size(name) + lax.axis_index(name)
    return index


def body(
    event_features,
    event_bins,
    positive,
    teacher_bank,
    in_weight,
    embedding_head_weight,
    membrane_decay_rate,
):
    per_device = positive.shape[0]
    bank_rows = teacher_bank.shape[0]
    onehot = (event_bins[:, None, :] == jnp.arange(TIME, dtype=jnp.int32)[None, :, None]).astype(
        jnp.bfloat16
    )
    binned = jnp.einsum(
        "ste,sec->stc", onehot, event_features, preferred_element_type=jnp.float32
    ).astype(jnp.bfloat16)
    flat_in = binned.reshape(per_device * TIME, C_IN)
    input_current = jnp.dot(flat_in, in_weight, preferred_element_type=jnp.float32).reshape(
        per_device, TIME, H
    )
    spike_train, leaky_neuron_backward = jax.vjp(
        partial(membrane_potential, membrane_decay_rate=membrane_decay_rate), input_current
    )
    spike_train_reduced = spike_train.astype(jnp.bfloat16)
    projected_embedding = jnp.dot(
        spike_train_reduced, embedding_head_weight, preferred_element_type=jnp.float32
    )
    length = jnp.sqrt(
        jnp.sum(projected_embedding * projected_embedding, axis=1, keepdims=True) + epsilon
    )
    query = projected_embedding / length
    query_low = query.astype(jnp.bfloat16)

    digits = jnp.stack([(positive >> 12) & 63, (positive >> 6) & 63, positive & 63], axis=1)
    code = jnp.zeros((per_device, CODE_COLS), jnp.bfloat16).at[:, :3].set(
        digits.astype(jnp.bfloat16)
    )
    gathered = jnp.concatenate([query_low, code], axis=1)
    for name in GATHER_ORDER:
        gathered = lax.all_gather(gathered, name, axis=0, tiled=True)
    gathered_query = gathered[:, :D]
    gathered_digits = gathered[:, D : D + 3].astype(jnp.int32)
    gathered_pos = (
        gathered_digits[:, 0] * 4096 + gathered_digits[:, 1] * 64 + gathered_digits[:, 2]
    )

    start_row = bank_index() * bank_rows
    inverse = 1.0 / jnp.sqrt(
        jnp.sum(jnp.square(teacher_bank.astype(jnp.float32)), axis=1) + epsilon
    )
    local_index = gathered_pos - start_row
    is_owner = (local_index >= 0) & (local_index < bank_rows)
    local_index = jnp.clip(local_index, 0, bank_rows - 1)

    cosine_affinity_matrix = (
        jnp.dot(gathered_query, teacher_bank.T, preferred_element_type=jnp.float32)
        * inverse[None, :]
        / sharpening_divisor
    )
    exponent = jnp.exp(cosine_affinity_matrix)
    weights = (exponent * inverse[None, :]).astype(jnp.bfloat16)
    partition_part = jnp.sum(exponent, axis=1)
    column = lax.broadcasted_iota(jnp.int32, cosine_affinity_matrix.shape, 1)
    picked = jnp.sum(
        jnp.where(column == local_index[:, None], cosine_affinity_matrix, 0.0), axis=1
    )
    pos_part = jnp.where(is_owner, picked, 0.0)

    stats = jnp.stack([partition_part, pos_part])
    for name in reversed(GATHER_ORDER):
        stats = lax.psum(stats, name)
    exponent_total = stats[0]
    matched_dot_value = stats[1]
    own_start = gathered_block_index() * per_device
    own_partition = lax.dynamic_slice_in_dim(exponent_total, own_start, per_device, 0)
    own_pos = lax.dynamic_slice_in_dim(matched_dot_value, own_start, per_device, 0)
    sample_loss = jnp.log(own_partition) - own_pos

    partial_sums = jnp.dot(weights, teacher_bank, preferred_element_type=jnp.float32)
    matched_entries = (
        jnp.take(teacher_bank, local_index, axis=0).astype(jnp.float32)
        * jnp.take(inverse, local_index)[:, None]
    )
    local_owned_rows = jnp.where(is_owner[:, None], matched_entries, 0.0)
    query_grad = (partial_sums / exponent_total[:, None] - local_owned_rows) / (
        sharpening_divisor * objective_divisor
    )
    for name in reversed(GATHER_ORDER):
        query_grad = lax.psum_scatter(query_grad, name, scatter_dimension=0, tiled=True)

    projection_gradient = (
        (query_grad - query * jnp.sum(query * query_grad, axis=1, keepdims=True)) / length
    ).astype(jnp.bfloat16)
    head_weight_piece = jnp.dot(
        spike_train_reduced.T, projection_gradient, preferred_element_type=jnp.float32
    )
    spike_train_gradient = jnp.dot(
        projection_gradient, embedding_head_weight.T, preferred_element_type=jnp.float32
    )
    (input_current_gradient,) = leaky_neuron_backward(spike_train_gradient)
    current_low = input_current_gradient.astype(jnp.bfloat16).reshape(per_device * TIME, H)
    in_part = jnp.dot(flat_in.T, current_low, preferred_element_type=jnp.float32)

    sizes = [lax.axis_size(name) for name in BANK_AXES]
    bank_size = sizes[0] * sizes[1] * sizes[2]
    in_share_rows = C_IN // bank_size
    head_share_rows = H // bank_size
    grads = jnp.concatenate(
        [
            in_part.reshape(bank_size, in_share_rows * H),
            head_weight_piece.reshape(bank_size, head_share_rows * D),
        ],
        axis=1,
    )
    order = [BANK_AXES.index(name) for name in reversed(GATHER_ORDER)]
    grads = (
        grads.reshape(*sizes, grads.shape[1])
        .transpose(*order, 3)
        .reshape(bank_size, grads.shape[1])
    )
    for name in reversed(GATHER_ORDER):
        grads = lax.psum_scatter(grads, name, scatter_dimension=0, tiled=True)
    grads = lax.psum(grads, "dp")
    in_grad = grads[0, : in_share_rows * H].reshape(in_share_rows, H)
    head_weight_gradient = grads[0, in_share_rows * H :].reshape(head_share_rows, D)
    return (sample_loss, in_grad, head_weight_gradient)


def split_mesh(mesh):
    devices = mesh.devices
    column = devices[:, 0]
    try:
        xs = sorted({int(d.coords[0]) for d in column})
        zs = sorted({int(d.coords[2]) for d in column})
        cs = sorted({int(d.core_on_chip) for d in column})
        nx, nz, nc = len(xs), len(zs), len(cs)
        ok = nx * nz * nc == column.shape[0]
        for b, d in enumerate(column):
            want = (b // (nz * nc), (b // nc) % nz, b % nc)
            got = (xs.index(int(d.coords[0])), zs.index(int(d.coords[2])), cs.index(int(d.core_on_chip)))
            ok = ok and want == got
    except (AttributeError, IndexError, TypeError):
        ok = False
    if not ok:
        nx, nz, nc = 1, 1, column.shape[0]
    return Mesh(devices.reshape(nx, nz, nc, devices.shape[1]), SAMPLE_AXES)


def solution(mesh):
    split = split_mesh(mesh)
    in_specs = (
        P(SAMPLE_AXES, None, None),
        P(SAMPLE_AXES, None),
        P(SAMPLE_AXES),
        P(BANK_AXES, None),
        P(),
        P(),
        P(),
    )
    out_specs = (P(SAMPLE_AXES), P(BANK_AXES, None), P(BANK_AXES, None))
    return jax.shard_map(body, mesh=split, in_specs=in_specs, out_specs=out_specs, check_vma=False)
```

time: 689 us -> 429 us (0.62)
  waiting for transfers between devices: 457 us -> 279 us
  blocking collectives: 132 us -> 59.1 us
    psum x1 -> x0, waiting for transfers between devices: 262 us -> none  [body(): in_full, head_full = lax.psum((in_part, head_weight_piece), ('bank', 'dp'))]
    unnamed x3 -> x10, waiting for transfers between devices: 0.05 us -> 122 us
    psum x1 -> x4, blocking collectives: 109 us -> 46.2 us  [the longest x3 28.9 us: body(): stats = lax.psum(stats, name)]
    reduce_scatter x1 -> x4, waiting for transfers between devices: 159 us -> 102 us  [the longest x3 84.7 us: body(): lax.psum_scatter(query_grad, name, scatter_dimension=0, tiled=True)]
    unnamed x1 -> x0, blocking collectives: 22.5 us -> none
    all_gather x1 -> x2, waiting for transfers between devices: 36.1 us -> 54.9 us  [body(): gathered = lax.all_gather(gathered, name, axis=0, tiled=True)]
    gather x2 -> x0, local copies, waits for them, and re-layouts: 16.2 us -> none  [score_block(): jnp.take_along_axis(cosine_affinity_matrix, block_local[:, None], axis=1)]
    all_gather x0 -> x1, blocking collectives: none -> 12.9 us  [body(): gathered = lax.all_gather(gathered, name, axis=0, tiled=True)]
  transfers between devices with their start and end apart: 3 -> 8, of which waited for: 3 -> 8; matrix products, arithmetic and copies ran while one was open for 3% -> 1% of each run, Pallas kernels for 0% -> 0%
where the time goes in v1:
time: 429 us; the launch traced here: 428 us
  waiting for transfers between devices  279 us (65%)
  blocking collectives  59.1 us (14%)
  local copies, waits for them, and re-layouts  30.7 us (7%)
  matrix products  27 us (6%)
  other arithmetic  16.1 us (4%)
  between operations  15.1 us (4%)
    unnamed x10, waiting for transfers between devices  122 us
    reduce_scatter x3, waiting for transfers between devices, body(): lax.psum_scatter(query_grad, name, scatter_dimension=0, tiled=True)  84.7 us
    all_gather x2, waiting for transfers between devices, body(): gathered = lax.all_gather(gathered, name, axis=0, tiled=True)  54.9 us
    psum x3, blocking collectives, body(): stats = lax.psum(stats, name)  28.9 us
    psum x1, blocking collectives, body(): grads = lax.psum(grads, 'dp')  17.3 us
    reduce_scatter x1, waiting for transfers between devices, body(): grads = lax.psum_scatter(grads, name, scatter_dimension=0, tiled=True)  17.3 us
    all_gather x1, blocking collectives, body(): gathered = lax.all_gather(gathered, name, axis=0, tiled=True)  12.9 us
    dot_general x1, matrix products, body(): jnp.dot(gathered_query, teacher_bank.T, preferred_element_type=jnp.float32)  10.4 us
  transfers between devices with their start and end apart: 8, of which 8 were waited for; matrix products, arithmetic and copies ran while one was open for 1% of the time, Pallas kernels for 0%

profile of v1, /device:TPU:2, one launch (start us, length us, event | category | flops | bytes accessed | tf_op | source)
XLA Modules:
  0.0 427.6 jit_solution(3524358908737334216)
XLA Ops:
  7.2 0.6 compare_reduce_fusion
  7.9 0.7 convert_bitcast_fusion.2
  8.6 1.0 convolution_convert_fusion
  9.6 0.6 copy-done.2
  10.3 1.1 fusion.8
  11.5 1.3 broadcast_multiply_fusion
  12.8 0.8 fusion.37
  13.6 1.1 multiply_reduce_fusion.2
  14.7 0.7 broadcast_select_fusion
  15.5 12.9 %all_gather.9 = bf16[64,1152]{1,0:T(8,128)(2,1)} all-gather(bf16[16,1152]{1,0:T(8,128)(2,1)S(1)} %fusion.12), channel_id=1, replica_groups=mesh['bx'=4,'bz'=8,'bc'=2,'dp'=4] {'bx'}, dimensions={0}, use_global_device_ids=true | all-gather | bytes 184320 | tf_op jit(solution)/shard_map/all_gather | solution.py:92
  28.4 41.6 %all-gather.3.cloned.1.call-done = bf16[512,1152]{1,0:T(8,128)(2,1)} async-done(((bf16[64,1152]{1,0:T(8,128)(2,1)}), bf16[512,1152]{1,0:T(8,128)(2,1)}) %all-gather.3.cloned.1.call-update) | async-done | bytes 1179664 | tf_op jit(solution)/shard_map/all_gather | solution.py:92
  70.1 3.1 multiply_reduce_fusion
  73.2 13.3 %all-gather.5.cloned.1.call-done = bf16[1024,1152]{1,0:T(8,128)(2,1)} async-done(((bf16[512,1152]{1,0:T(8,128)(2,1)}), bf16[1024,1152]{1,0:T(8,128)(2,1)}) %all-gather.5.cloned.1.call-update) | async-done | bytes 2359312 | tf_op jit(solution)/shard_map/all_gather | solution.py:92
  86.5 1.0 slice_convert_fusion
  87.5 1.1 fusion.67
  88.7 0.4 fusion.7
  89.3 7.7 %gather_fusion = bf16[1024,1024]{1,0:T(8,128)(2,1)S(1)} fusion(bf16[2048,1024]{1,0:T(8,128)(2,1)} %param.12, s32[1024]{0:T(1024)S(1)} %broadcast_clamp_fusion), kind=kCustom, calls=%fused_computation | custom fusion | bytes 4198400 | tf_op jit(solution)/shard_map/jit(_take)/gather | solution.py:133
  97.0 6.2 %gather_fusion.1 = f32[1024]{0:T(1024)S(1)} fusion(f32[2048]{0:T(1024)S(1)} %add_rsqrt_fusion, s32[1024]{0:T(1024)S(1)} %broadcast_clamp_fusion), kind=kCustom, calls=%fused_computation.1 | custom fusion | bytes 12288 | tf_op jit(solution)/shard_map/jit(_take)/gather | solution.py:134
  103.1 10.4 %exponential_reduce_fusion = (f32[1024]{0:T(1024)S(1)}, f32[1024]{0:T(1024)S(1)}, f32[1024,2048]{1,0:T(8,128)}) fusion(f32[2048]{0:T(1024)S(1)} %add_rsqrt_fusion, s32[1024]{0:T(1024)S(1)} %get-tuple-element.18, bf16[2048,1024]{1,0:T(8,128)(2,1)} %param.12, bf16[1024,1152]{1,0:T(8,128)(2,1)} %all-gather.5.cloned.1.call-done), kind=kOutput, calls=%fused_computation.7 | convolution fusion | flops 4307548160 | bytes 14700544 | tf_op jit(solution)/shard_map/dot_general | solution.py:108
  113.6 2.5 psum.28
  116.1 17.7 %psum.29 = f32[2,1024]{1,0:T(2,128)S(1)} all-reduce(f32[2,1024]{1,0:T(2,128)S(1)} %psum.28), channel_id=1, replica_groups=mesh['bx'=4,'bz'=8,'bc'=2,'dp'=4] {'bz'}, use_global_device_ids=true, to_apply=%region_6.7 | all-reduce | flops 2048 | bytes 16384 | tf_op jit(solution)/shard_map/psum | solution.py:123
  133.8 8.7 %psum.30 = f32[2,1024]{1,0:T(2,128)S(1)} all-reduce(f32[2,1024]{1,0:T(2,128)S(1)} %psum.29), channel_id=1, replica_groups=mesh['bx'=4,'bz'=8,'bc'=2,'dp'=4] {'bx'}, use_global_device_ids=true, to_apply=%region_7.8 | all-reduce | flops 2048 | bytes 16384 | tf_op jit(solution)/shard_map/psum | solution.py:123
  142.5 0.6 fusion.72
  143.1 1.1 copy.43
  144.2 1.3 select_reduce_fusion.1
  145.5 10.1 %subtract_multiply_fusion = f32[1024,1024]{1,0:T(8,128)} fusion(f32[1024]{0:T(1024)S(1)} %select_reduce_fusion.1, bf16[1024,1024]{1,0:T(8,128)(2,1)S(1)} %gather_fusion, f32[1024]{0:T(1024)S(1)} %bitcast.193, pred[1024]{0:T(1024)(128)(4,1)S(1)} %get-tuple-element.25, pred[1024]{0:T(1024)(128)(4,1)S(1)} %and_reduce_fusion, bf16[2048,1024]{1,0:T(8,128)(2,1)} %param.12, ...), kind=kOutput, calls=%fused_computation.9 | convolution fusion | flops 4310695936 | bytes 18892800 | tf_op jit(solution)/shard_map/dot_general | solution.py:131
  155.7 15.9 %reduce-scatter.5.cloned.1.call-done = f32[512,1024]{1,0:T(8,128)} async-done(((f32[1024,1024]{1,0:T(8,128)}), f32[512,1024]{1,0:T(8,128)}) %reduce-scatter.5.cloned.1.call-update) | async-done | bytes 2097168 | tf_op jit(solution)/shard_map/reduce_scatter | solution.py:141
  171.7 46.5 %reduce-scatter.7.cloned.1.call-done = f32[64,1024]{1,0:T(8,128)} async-done(((f32[512,1024]{1,0:T(8,128)}), f32[64,1024]{1,0:T(8,128)}) %reduce-scatter.7.cloned.1.call-update) | async-done | bytes 262160 | tf_op jit(solution)/shard_map/reduce_scatter | solution.py:141
  218.4 22.3 %reduce-scatter.9.cloned.1.call-done = f32[16,1024]{1,0:T(8,128)} async-done(((f32[64,1024]{1,0:T(8,128)}), f32[16,1024]{1,0:T(8,128)}) %reduce-scatter.9.cloned.1.call-update) | async-done | bytes 65552 | tf_op jit(solution)/shard_map/reduce_scatter | solution.py:141
  240.7 1.0 multiply_reduce_fusion.1
  241.7 0.5 copy-done.7
  242.2 2.7 fusion.62
  244.9 3.1 concatenate.15
  248.0 2.7 copy.46
  250.7 0.4 convolution_multiply_fusion
  252.1 2.2 maximum_bitcast_fusion
  254.3 1.9 reshape.130
  256.3 17.3 %reduce-scatter.11.cloned.1.call-done = f32[32,9216]{1,0:T(8,128)} async-done(((f32[64,9216]{1,0:T(8,128)}), f32[32,9216]{1,0:T(8,128)}) %reduce-scatter.11.cloned.1.call-update) | async-done | bytes 1179664 | tf_op jit(solution)/shard_map/reduce_scatter | solution.py:174
  273.6 0.6 dynamic-slice.9
  274.9 78.9 %all-reduce.14.cloned.1.call-done = f32[32,9216]{1,0:T(8,128)} async-done(((f32[32,9216]{1,0:T(8,128)}), f32[32,9216]{1,0:T(8,128)}) %all-reduce.14.cloned.1.call-update) | async-done | bytes 1179664
  353.8 1.7 constant_dynamic-slice_fusion.1
  355.5 0.6 dynamic-slice.11
  356.0 1.2 subtract_bitcast_fusion
  357.3 43.2 %all-reduce.16.cloned.1.call-done = f32[4,9216]{1,0:T(4,128)} async-done(((f32[4,9216]{1,0:T(4,128)}), f32[4,9216]{1,0:T(4,128)}) %all-reduce.16.cloned.1.call-update) | async-done | bytes 147472
  400.5 1.6 constant_dynamic-slice_fusion
  402.1 17.3 %psum.31 = f32[1,9216]{1,0:T(1,128)S(1)} all-reduce(f32[1,9216]{1,0:T(1,128)S(1)} %constant_dynamic-slice_fusion), channel_id=1, replica_groups=mesh['bx'=4,'bz'=8,'bc'=2,'dp'=4] {'dp'}, use_global_device_ids=true, to_apply=%region_15.16 | all-reduce | flops 9216 | bytes 73728 | tf_op jit(solution)/shard_map/psum | solution.py:175
  419.5 0.6 reshape_squeeze.6
  420.1 0.6 reshape_squeeze.7
  (57 shorter events, 2.4 us)
Async XLA Ops:
  7.2 6.4 %copy-start = (bf16[512,1024]{1,0:T(8,128)(2,1)S(1)}, bf16[512,1024]{1,0:T(8,128)(2,1)}, u32[]{:S(2)}) copy-start(bf16[512,1024]{1,0:T(8,128)(2,1)} %param.14) | copy-start | bytes 3145732
  7.2 62.9 %all-gather.3.cloned.1.call-start = ((), (), s32[]{:S(2)}) async-start(), calls=%async_computation.4 | async-start | bytes 1327104 | tf_op jit(solution)/shard_map/all_gather | solution.py:92
  9.6 0.6 copy-start.2
  28.4 58.1 %all-gather.5.cloned.1.call-start = ((), (), s32[]{:S(2)}) async-start(), calls=%async_computation.5 | async-start | bytes 3538944 | tf_op jit(solution)/shard_map/all_gather | solution.py:92
  70.1 101.5 %reduce-scatter.5.cloned.1.call-start = ((), (), s32[]{:S(2)}) async-start(), calls=%async_computation.6 | async-start | bytes 6291456 | tf_op jit(solution)/shard_map/reduce_scatter | solution.py:141
  143.1 12.5 %copy-start.6 = (f32[1,1024]{1,0:T(1,128)}, f32[1,1024]{1,0:T(1,128)S(1)}, u32[]{:S(2)}) copy-start(f32[1,1024]{1,0:T(1,128)S(1)} %get-tuple-element.40) | copy-start | bytes 12292
  155.6 86.6 %copy-start.4 = (f32[512]{0:T(512)S(1)}, f32[512]{0:T(512)}, u32[]{:S(2)}) copy-start(f32[512]{0:T(512)} %param.15) | copy-start | bytes 6148
  155.6 62.5 %reduce-scatter.7.cloned.1.call-start = ((), (), s32[]{:S(2)}) async-start(), calls=%async_computation.7 | async-start | bytes 2359296 | tf_op jit(solution)/shard_map/reduce_scatter | solution.py:141
  171.6 69.0 %reduce-scatter.9.cloned.1.call-start = ((), (), s32[]{:S(2)}) async-start(), calls=%async_computation.8 | async-start | bytes 327680 | tf_op jit(solution)/shard_map/reduce_scatter | solution.py:141
  218.2 55.4 %reduce-scatter.11.cloned.1.call-start = ((), (), s32[]{:S(2)}) async-start(), calls=%async_computation.9 | async-start | bytes 3538944 | tf_op jit(solution)/shard_map/reduce_scatter | solution.py:174
  241.7 0.5 copy-start.7
  244.9 5.8 %copy-start.1 = (f32[16,1024]{1,0:T(8,128)S(1)}, f32[16,1024]{1,0:T(8,128)}, u32[]{:S(2)}) copy-start(f32[16,1024]{1,0:T(8,128)} %reduce-scatter.9.cloned.1.call-done) | copy-start | bytes 196612
  244.9 6.2 %copy-start.5 = (f32[512]{0:T(512)S(1)}, f32[512]{0:T(512)}, u32[]{:S(2)}) copy-start(f32[512]{0:T(512)} %get-tuple-element.42) | copy-start | bytes 6148
  248.0 2.7 copy-start.8
  248.0 3.5 copy-start.3
  254.3 19.3 %copy-start.10 = (u32[256]{0:T(256)S(1)}, u32[256]{0:T(256)}, u32[]{:S(2)}) copy-start(u32[256]{0:T(256)} %constant.154) | copy-start | bytes 3076
  254.3 101.2 %copy-start.9 = (u32[256]{0:T(256)S(1)}, u32[256]{0:T(256)}, u32[]{:S(2)}) copy-start(u32[256]{0:T(256)} %constant.158) | copy-start | bytes 3076
  256.2 97.5 %all-reduce.14.cloned.1.call-start = ((), (), s32[]{:S(2)}) async-start(), calls=%async_computation.10 | async-start | bytes 2359296
  273.6 126.9 %all-reduce.16.cloned.1.call-start = ((), (), s32[]{:S(2)}) async-start(), calls=%async_computation.11 | async-start | bytes 294912
Sparse Core Ops, SparseCore 0:
  28.5 41.4 all-gather.2
  71.8 14.6 all-gather.4
  155.7 15.8 reduce-scatter.4
  174.0 44.0 reduce-scatter.6
  220.5 20.1 reduce-scatter.8
  256.3 17.1 reduce-scatter.10
  275.9 77.8 all-reduce.13
  356.1 44.3 all-reduce.15
